TPU v7x, 256 devices: a whole 4x4x8 slice. The times are simulated.
256 devices in a mesh: dp: 32 (over z, y), tensor: 8 (over x, core).
Axes of the slice: x: 4, y: 4, z: 8, core: 2. Of those that a mesh axis runs over, the one named last changes fastest.
Arguments:
- tokens: bfloat16 [4096, 4096], P('dp', 'tensor'), may hold values from -6 to 6
- grad_out: bfloat16 [4096, 4096], P('dp', 'tensor'), may hold values from -6 to 6
- gate_blocks: int32 [8, 32], P('tensor'), may hold values from -1 to 447, as said below
- gate_values: bfloat16 [8, 32, 128, 128], P('tensor'), may hold values from -0.375 to 0.375
- up_blocks: int32 [8, 32], P('tensor'), may hold values from -1 to 447, as said below
- up_values: bfloat16 [8, 32, 128, 128], P('tensor'), may hold values from -0.375 to 0.375
- down_blocks: int32 [8, 32], P('tensor'), may hold values from -1 to 447, as said below
- down_values: bfloat16 [8, 32, 128, 128], P('tensor'), may hold values from -0.1875 to 0.1875
Outputs:
- mixed: bfloat16 [4096, 4096], P('dp', 'tensor')
- grad_tokens: bfloat16 [4096, 4096], P('dp', 'tensor')
- grad_gate: float32 [8, 32, 128, 128], P('tensor', 'dp')
- grad_up: float32 [8, 32, 128, 128], P('tensor', 'dp')
- grad_down: float32 [8, 32, 128, 128], P('tensor', 'dp')
Inputs may be any that keep to these rules, and one draw needn't show every extreme that they name: `gate_blocks`: each row lists distinct block numbers of one tensor shard in its first slots and -1 in the rest; a row has 16 to 32 listed blocks, one row has exactly 32 and another exactly 16. `up_blocks`: as for gate_blocks, drawn apart. `down_blocks`: as for gate_blocks, drawn apart.
All inputs are finite; a program needn't handle non-finite values.
Results may differ from a plain program's by a relative error of at most 0.015.
Values may be sent and summed in bfloat16 or wider, within the bound.
No kernel may reach another device: no remote copies, remote signals or barrier semaphores. Data moves between devices by JAX's collectives and lax.ppermute only.
A program may use at most 64 MiB of HBM per device.

v0:
```python
import jax
import jax.numpy as jnp
from jax import lax
from jax.sharding import PartitionSpec as P

FF = 14336


def locate(blocks, feature_count):
    flat = blocks[0]
    weight = (flat >= 0).astype(jnp.float32)
    safe = jnp.maximum(flat, 0)
    return (safe // feature_count, safe % feature_count, weight)


def one_hot(targets, weight, count):
    return (targets[:, None] == jnp.arange(count)[None, :]).astype(jnp.float32) * weight[:, None]


def spread(product, table):
    return jnp.einsum("tsn,sc->tcn", product, table, precision=lax.Precision.HIGHEST)


def select(source, position):
    return jnp.take(source, position, axis=1)


def forward_blocks(rows_in, values):
    return jnp.einsum("tsk,skn->tsn", rows_in, values, preferred_element_type=jnp.float32)


def backward_blocks(rows_in, values):
    return jnp.einsum("tsn,skn->tsk", rows_in, values, preferred_element_type=jnp.float32)


def slot_term(left, right, weight):
    product = jnp.einsum("tsk,tsn->skn", left, right, preferred_element_type=jnp.float32)
    return product * weight[:, None, None]


def body(
    tokens, grad_out, gate_blocks, gate_values, up_blocks, up_values, down_blocks, down_values
):
    gathered_x, gathered_dy = (
        lax.all_gather(tokens, "tensor", axis=1, tiled=True),
        lax.all_gather(grad_out, "tensor", axis=1, tiled=True),
    )
    tok_rows, feature_width = gathered_x.shape
    block_size = gate_values.shape[-1]
    feature_count = feature_width // block_size
    hidden_count = FF // (block_size * lax.axis_size("tensor"))
    inputs = gathered_x.reshape(tok_rows, feature_count, block_size)
    upstream = gathered_dy.reshape(tok_rows, feature_count, block_size)
    gate_hid, gate_feat, gate_live = locate(gate_blocks, feature_count)
    up_hid, up_feat, up_live = locate(up_blocks, feature_count)
    down_hid, down_feat, down_live = locate(down_blocks, feature_count)
    gate_rows = select(inputs, gate_feat)
    up_rows = select(inputs, up_feat)
    gate_pre = spread(
        forward_blocks(gate_rows, gate_values[0]), one_hot(gate_hid, gate_live, hidden_count)
    )
    up_pre = spread(forward_blocks(up_rows, up_values[0]), one_hot(up_hid, up_live, hidden_count))
    sigma_gate = jax.nn.sigmoid(gate_pre)
    activated = gate_pre * sigma_gate
    hidden = (activated * up_pre).astype(jnp.bfloat16)
    hidden_rows = select(hidden, down_hid)
    mixed_part = spread(
        forward_blocks(hidden_rows, down_values[0]), one_hot(down_feat, down_live, feature_count)
    )
    mixed_part = mixed_part.reshape(tok_rows, feature_width)
    upstream_rows = select(upstream, down_feat)
    mixed = lax.psum_scatter(
        mixed_part.astype(jnp.bfloat16), "tensor", scatter_dimension=1, tiled=True
    )
    hidden_grad = spread(
        backward_blocks(upstream_rows, down_values[0]), one_hot(down_hid, down_live, hidden_count)
    )
    gate_delta = (hidden_grad * up_pre * sigma_gate * (1.0 + gate_pre * (1.0 - sigma_gate))).astype(
        jnp.bfloat16
    )
    up_delta = (hidden_grad * activated).astype(jnp.bfloat16)
    gate_delta_rows = select(gate_delta, gate_hid)
    up_delta_rows = select(up_delta, up_hid)
    input_part = spread(
        backward_blocks(gate_delta_rows, gate_values[0]),
        one_hot(gate_feat, gate_live, feature_count),
    )
    input_part = input_part + spread(
        backward_blocks(up_delta_rows, up_values[0]), one_hot(up_feat, up_live, feature_count)
    )
    input_part = input_part.reshape(tok_rows, feature_width)
    gate_term = slot_term(gate_rows, gate_delta_rows, gate_live)
    up_term = slot_term(up_rows, up_delta_rows, up_live)
    down_term = slot_term(hidden_rows, upstream_rows, down_live)
    grad_gate, grad_up, grad_down = (
        lax.psum_scatter(term.astype(jnp.bfloat16), "dp", scatter_dimension=0, tiled=True).astype(
            jnp.float32
        )[None]
        for term in (gate_term, up_term, down_term)
    )
    grad_tokens = lax.psum_scatter(
        input_part.astype(jnp.bfloat16), "tensor", scatter_dimension=1, tiled=True
    )
    return (mixed, grad_tokens, grad_gate, grad_up, grad_down)


def solution(mesh):
    in_specs = (
        P("dp", "tensor"),
        P("dp", "tensor"),
        P("tensor", None),
        P("tensor", None, None, None),
        P("tensor", None),
        P("tensor", None, None, None),
        P("tensor", None),
        P("tensor", None, None, None),
    )
    out_specs = (
        P("dp", "tensor"),
        P("dp", "tensor"),
        P("tensor", "dp", None, None),
        P("tensor", "dp", None, None),
        P("tensor", "dp", None, None),
    )
    return jax.shard_map(body, mesh=mesh, in_specs=in_specs, out_specs=out_specs, check_vma=False)
```

profile of v0, /device:TPU:8, one launch (start us, length us, event | category | flops | bytes accessed | tf_op | source)
XLA Modules:
  0.0 825.7 jit_solution(16852433310537458351)
XLA Ops:
  7.2 1.7 copy.39
  9.0 1.7 copy.47
  14.9 24.2 %all-gather.3.cloned.1.call-done = bf16[128,4096]{0,1:T(8,128)(2,1)} async-done(((bf16[128,512]{0,1:T(8,128)(2,1)}), bf16[128,4096]{0,1:T(8,128)(2,1)}) %all-gather.3.cloned.1.call-update) | async-done | bytes 1048592 | tf_op jit(solution)/shard_map/all_gather | solution.py:45
  39.1 1.6 copy.40
  40.7 26.5 %all-gather.5.cloned.1.call-done = bf16[128,4096]{0,1:T(8,128)(2,1)} async-done(((bf16[128,512]{0,1:T(8,128)(2,1)}), bf16[128,4096]{0,1:T(8,128)(2,1)}) %all-gather.5.cloned.1.call-update) | async-done | bytes 1048592 | tf_op jit(solution)/shard_map/all_gather | solution.py:46
  67.2 2.3 copy.48
  69.5 1.7 gather_fusion.1
  71.2 1.7 gather_fusion
  72.8 3.0 gather_fusion.3
  76.3 2.2 fusion.10
  79.1 2.2 fusion.8
  82.3 2.2 fusion.4
  85.6 1.7 gather_fusion.4
  87.2 3.2 multiply_convert_fusion.2
  90.7 1.7 gather_fusion.2
  92.4 3.2 multiply_convert_fusion
  95.7 1.6 gather_fusion.5
  97.3 3.3 multiply_convert_fusion.1
  101.2 3.0 fusion.14
  104.2 1.4 copy.90
  105.7 2.3 convolution_bitcast_fusion
  108.9 3.0 fusion
  111.9 3.1 add_convert_fusion
  115.0 1.4 copy.89
  116.5 190.5 %reduce-scatter.10.cloned.1.call-done = bf16[1,128,128]{2,1,0:T(8,128)(2,1)} async-done(((bf16[32,128,128]{2,1,0:T(8,128)(2,1)}), bf16[1,128,128]{2,1,0:T(8,128)(2,1)}) %reduce-scatter.10.cloned.1.call-update) | async-done | bytes 32784 | tf_op jit(solution)/shard_map/reduce_scatter | solution.py:96
  307.0 1.4 bitcast_convert_fusion.2
  308.4 217.8 %reduce-scatter.14.cloned.1.call-done = bf16[1,128,128]{2,1,0:T(8,128)(2,1)} async-done(((bf16[32,128,128]{2,1,0:T(8,128)(2,1)}), bf16[1,128,128]{2,1,0:T(8,128)(2,1)}) %reduce-scatter.14.cloned.1.call-update) | async-done | bytes 32784 | tf_op jit(solution)/shard_map/reduce_scatter | solution.py:96
  526.2 1.4 bitcast_convert_fusion
  527.6 217.8 %reduce-scatter.12.cloned.1.call-done = bf16[1,128,128]{2,1,0:T(8,128)(2,1)} async-done(((bf16[32,128,128]{2,1,0:T(8,128)(2,1)}), bf16[1,128,128]{2,1,0:T(8,128)(2,1)}) %reduce-scatter.12.cloned.1.call-update) | async-done | bytes 32784 | tf_op jit(solution)/shard_map/reduce_scatter | solution.py:96
  745.4 1.4 bitcast_convert_fusion.1
  746.8 35.4 %reduce-scatter.6.cloned.1.call-done = bf16[128,512]{1,0:T(8,128)(2,1)} async-done(((bf16[128,4096]{1,0:T(8,128)(2,1)}), bf16[128,512]{1,0:T(8,128)(2,1)}) %reduce-scatter.6.cloned.1.call-update) | async-done | bytes 131088 | tf_op jit(solution)/shard_map/reduce_scatter | solution.py:72
  782.2 36.7 %reduce-scatter.8.cloned.1.call-done = bf16[128,512]{1,0:T(8,128)(2,1)} async-done(((bf16[128,4096]{1,0:T(8,128)(2,1)}), bf16[128,512]{1,0:T(8,128)(2,1)}) %reduce-scatter.8.cloned.1.call-update) | async-done | bytes 131088 | tf_op jit(solution)/shard_map/reduce_scatter | solution.py:101
  (56 shorter events, 9.0 us)
Async XLA Ops:
  7.2 74.2 %copy-start = (bf16[1,32,128,128]{3,2,1,0:T(8,128)(2,1)S(1)}, bf16[1,32,128,128]{3,2,1,0:T(8,128)(2,1)}, u32[]{:S(2)}) copy-start(bf16[1,32,128,128]{3,2,1,0:T(8,128)(2,1)} %param.19) | copy-start | bytes 3145732
  7.2 31.9 %all-gather.3.cloned.1.call-start = ((), (), s32[]{:S(2)}) async-start(), calls=%async_computation.5 | async-start | bytes 1179648 | tf_op jit(solution)/shard_map/all_gather | solution.py:45
  9.0 58.3 %all-gather.5.cloned.1.call-start = ((), (), s32[]{:S(2)}) async-start(), calls=%async_computation.7 | async-start | bytes 1179648 | tf_op jit(solution)/shard_map/all_gather | solution.py:46
  10.7 296.2 %reduce-scatter.10.cloned.1.call-start = ((), (), s32[]{:S(2)}) async-start(), calls=%async_computation.9 | async-start | bytes 1081344 | tf_op jit(solution)/shard_map/reduce_scatter | solution.py:96
  71.2 4.6 copy-start.2
  72.8 3.0 copy-start.8
  76.3 2.3 copy-start.1
  76.3 2.3 copy-start.5
  79.1 2.3 copy-start.6
  90.5 435.7 %reduce-scatter.14.cloned.1.call-start = ((), (), s32[]{:S(2)}) async-start(), calls=%async_computation.11 | async-start | bytes 1081344 | tf_op jit(solution)/shard_map/reduce_scatter | solution.py:96
  95.6 649.8 %reduce-scatter.12.cloned.1.call-start = ((), (), s32[]{:S(2)}) async-start(), calls=%async_computation.10 | async-start | bytes 1081344 | tf_op jit(solution)/shard_map/reduce_scatter | solution.py:96
  97.3 3.4 copy-start.7
  100.6 681.5 %reduce-scatter.6.cloned.1.call-start = ((), (), s32[]{:S(2)}) async-start(), calls=%async_computation.6 | async-start | bytes 1179648 | tf_op jit(solution)/shard_map/reduce_scatter | solution.py:72
  105.6 2.3 copy-start.3
  105.6 713.2 %reduce-scatter.8.cloned.1.call-start = ((), (), s32[]{:S(2)}) async-start(), calls=%async_computation.8 | async-start | bytes 1179648 | tf_op jit(solution)/shard_map/reduce_scatter | solution.py:101
  105.7 2.3 copy-start.4
Sparse Core Ops, SparseCore 0:
  10.4 28.6 all-gather.2
  41.5 25.6 all-gather.4
  90.6 216.3 reduce-scatter.9
  310.6 215.4 reduce-scatter.13
  529.8 215.5 reduce-scatter.11
  748.4 33.7 reduce-scatter.5
  785.3 33.5 reduce-scatter.7
where the time goes:
time: 826 us
  waiting for transfers between devices  749 us (91%)
  matrix products  31 us (4%)
  local copies, waits for them, and re-layouts  21.4 us (3%)
  between operations  14.4 us (2%)
  other arithmetic  9.27 us (1%)
    reduce_scatter x3, waiting for transfers between devices, body(): lax.psum_scatter(term.astype(jnp.bfloat16), 'dp', scatter_dimension=0, ti...  626 us
    reduce_scatter x1, waiting for transfers between devices, body(): lax.psum_scatter(input_part.astype(jnp.bfloat16), 'tensor', scatter_dimen...  36.7 us
    reduce_scatter x1, waiting for transfers between devices, body(): lax.psum_scatter(mixed_part.astype(jnp.bfloat16), 'tensor', scatter_dimen...  35.4 us
    all_gather x1, waiting for transfers between devices, body(): lax.all_gather(grad_out, 'tensor', axis=1, tiled=True)  26.5 us
    all_gather x1, waiting for transfers between devices, body(): lax.all_gather(tokens, 'tensor', axis=1, tiled=True)  24.2 us
  transfers between devices with their start and end apart: 7, of which 7 were waited for; matrix products, arithmetic and copies ran while one was open for 4% of the time, Pallas kernels for 0%

commit v1 on v0

--- a/solution.py
+++ b/solution.py
@@ -4,6 +4,27 @@
 from jax.sharding import PartitionSpec as P
 
 FF = 14336
+
+
+def collect(x, axis, dim):
+    size, mine, extent = (lax.axis_size(axis), lax.axis_index(axis), x.shape[dim])
+    upward = [(i, (i + 1) % size) for i in range(size)]
+    left = [(i, (i - 1) % size) for i in range(size)]
+    result = jnp.zeros((*x.shape[:dim], size * extent, *x.shape[dim + 1 :]), x.dtype)
+    result = lax.dynamic_update_slice_in_dim(result, x, mine * extent, axis=dim)
+    from_left = from_right = x
+    half = size // 2
+    for lap in range(1, half + 1):
+        from_left = lax.ppermute(from_left, axis, upward)
+        result = lax.dynamic_update_slice_in_dim(
+            result, from_left, (mine - lap) % size * extent, axis=dim
+        )
+        if lap < size - half:
+            from_right = lax.ppermute(from_right, axis, left)
+            result = lax.dynamic_update_slice_in_dim(
+                result, from_right, (mine + lap) % size * extent, axis=dim
+            )
+    return result
 
 
 def locate(blocks, feature_count):
@@ -42,7 +63,7 @@
     tokens, grad_out, gate_blocks, gate_values, up_blocks, up_values, down_blocks, down_values
 ):
     gathered_x, gathered_dy = (
-        lax.all_gather(tokens, "tensor", axis=1, tiled=True),
+        collect(tokens, "tensor", 1),
         lax.all_gather(grad_out, "tensor", axis=1, tiled=True),
     )
     tok_rows, feature_width = gathered_x.shape

time: 826 us -> 800 us (0.969)
  waiting for transfers between devices: 749 us -> 712 us
  starting transfers between devices: 0.47 us -> 9.52 us
    all_gather x1, waiting for transfers between devices: 26.5 us -> 0.01 us  [body(): lax.all_gather(grad_out, 'tensor', axis=1, tiled=True)]
    all_gather x1 -> x0, waiting for transfers between devices: 24.2 us -> none  [body(): lax.all_gather(tokens, 'tensor', axis=1, tiled=True)]
    ppermute x0 -> x7, waiting for transfers between devices: none -> 11.6 us  [the longest x4 11.2 us: collect(): from_left = lax.ppermute(from_left, axis, upward)]
    ppermute x0 -> x7, starting transfers between devices: none -> 8.87 us  [the longest x3 8.83 us: collect(): from_right = lax.ppermute(from_right, axis, left)]
  transfers between devices with their start and end apart: 7 -> 13, of which waited for: 7 -> 9; matrix products, arithmetic and copies ran while one was open for 4% -> 6% of each run, Pallas kernels for 0% -> 0%
where the time goes in v1:
time: 800 us; the launch traced here: 799 us
  waiting for transfers between devices  712 us (89%)
  matrix products  34 us (4%)
  local copies, waits for them, and re-layouts  20.7 us (3%)
  between operations  14.6 us (2%)
  starting transfers between devices  9.52 us (1%)
  other arithmetic  8.62 us (1%)
    reduce_scatter x3, waiting for transfers between devices, body(): lax.psum_scatter(term.astype(jnp.bfloat16), 'dp', scatter_dimension=0, ti...  628 us
    reduce_scatter x1, waiting for transfers between devices, body(): lax.psum_scatter(mixed_part.astype(jnp.bfloat16), 'tensor', scatter_dimen...  36.6 us
    reduce_scatter x1, waiting for transfers between devices, body(): lax.psum_scatter(input_part.astype(jnp.bfloat16), 'tensor', scatter_dimen...  35.5 us
    dot_general x6, matrix products, spread(): jnp.einsum('tsn,sc->tcn', product, table, precision=lax.Precision.HIGHEST)  17.8 us
  transfers between devices with their start and end apart: 13, of which 9 were waited for; matrix products, arithmetic and copies ran while one was open for 6% of the time, Pallas kernels for 0%

profile of v1, /device:TPU:8, one launch (start us, length us, event | category | flops | bytes accessed | tf_op | source)
XLA Modules:
  0.0 799.3 jit_solution(5134314741263809263)
XLA Ops:
  8.4 2.9 collective-permute-start.1
  11.3 1.7 copy.51
  16.8 2.9 collective-permute-start.3
  19.8 2.6 collective-permute-done.2
  22.4 3.0 collective-permute-start.5
  25.4 2.6 collective-permute-done.4
  28.5 6.0 collective-permute-done.6
  35.2 1.7 gather_fusion
  36.9 1.6 gather_fusion.1
  38.5 1.7 convolution_bitcast_fusion.5
  40.2 3.2 fusion.10
  44.0 3.2 fusion.8
  47.2 2.3 copy.52
  49.6 2.9 gather_fusion.3
  52.5 2.1 convolution_bitcast_fusion.2
  54.6 2.2 fusion.4
  57.9 1.7 gather_fusion.5
  59.6 3.2 multiply_convert_fusion.1
  63.0 1.7 gather_fusion.4
  64.7 3.2 multiply_convert_fusion.2
  68.0 1.6 gather_fusion.2
  69.6 3.3 multiply_convert_fusion
  75.1 3.0 fusion
  78.1 3.1 add_convert_fusion
  81.3 1.4 copy.93
  83.7 3.0 fusion.14
  86.7 1.4 copy.94
  88.2 192.3 %reduce-scatter.12.cloned.1.call-done = bf16[1,128,128]{2,1,0:T(8,128)(2,1)} async-done(((bf16[32,128,128]{2,1,0:T(8,128)(2,1)}), bf16[1,128,128]{2,1,0:T(8,128)(2,1)}) %reduce-scatter.12.cloned.1.call-update) | async-done | bytes 32784 | tf_op jit(solution)/shard_map/reduce_scatter | solution.py:117
  281.8 218.0 %reduce-scatter.10.cloned.1.call-done = bf16[1,128,128]{2,1,0:T(8,128)(2,1)} async-done(((bf16[32,128,128]{2,1,0:T(8,128)(2,1)}), bf16[1,128,128]{2,1,0:T(8,128)(2,1)}) %reduce-scatter.10.cloned.1.call-update) | async-done | bytes 32784 | tf_op jit(solution)/shard_map/reduce_scatter | solution.py:117
  501.2 217.8 %reduce-scatter.14.cloned.1.call-done = bf16[1,128,128]{2,1,0:T(8,128)(2,1)} async-done(((bf16[32,128,128]{2,1,0:T(8,128)(2,1)}), bf16[1,128,128]{2,1,0:T(8,128)(2,1)}) %reduce-scatter.14.cloned.1.call-update) | async-done | bytes 32784 | tf_op jit(solution)/shard_map/reduce_scatter | solution.py:117
  720.4 35.5 %reduce-scatter.8.cloned.1.call-done = bf16[128,512]{1,0:T(8,128)(2,1)} async-done(((bf16[128,4096]{1,0:T(8,128)(2,1)}), bf16[128,512]{1,0:T(8,128)(2,1)}) %reduce-scatter.8.cloned.1.call-update) | async-done | bytes 131088 | tf_op jit(solution)/shard_map/reduce_scatter | solution.py:122
  755.9 36.6 %reduce-scatter.6.cloned.1.call-done = bf16[128,512]{1,0:T(8,128)(2,1)} async-done(((bf16[128,4096]{1,0:T(8,128)(2,1)}), bf16[128,512]{1,0:T(8,128)(2,1)}) %reduce-scatter.6.cloned.1.call-update) | async-done | bytes 131088 | tf_op jit(solution)/shard_map/reduce_scatter | solution.py:93
  (75 shorter events, 15.2 us)
Async XLA Ops:
  7.2 36.3 %copy-start = (bf16[1,32,128,128]{3,2,1,0:T(8,128)(2,1)S(1)}, bf16[1,32,128,128]{3,2,1,0:T(8,128)(2,1)}, u32[]{:S(2)}) copy-start(bf16[1,32,128,128]{3,2,1,0:T(8,128)(2,1)} %param.17) | copy-start | bytes 3145732
  7.2 40.0 %all-gather.2.cloned.1.call-start = ((), (), s32[]{:S(2)}) async-start(), calls=%async_computation.6 | async-start | bytes 1179648 | tf_op jit(solution)/shard_map/all_gather | solution.py:67
  8.3 8.5 %collective-permute-start = (bf16[128,512]{0,1:T(8,128)(2,1)S(1)}, bf16[128,512]{0,1:T(8,128)(2,1)S(1)}, u32[]{:S(2)}, u32[]{:S(2)}) collective-permute-start(bf16[128,512]{0,1:T(8,128)(2,1)S(1)} %copy.41), channel_id=1, source_target_pairs={{0,1},{1,2},{2,3},{3,4},{4,5},{5,6},{6,7},{7,0},{8,9},{9,10},{10,1... | collective-permute-start | bytes 393224 | tf_op jit(solution)/shard_map/ppermute | solution.py:18
  8.4 8.5 %collective-permute-start.1 = (bf16[128,512]{0,1:T(8,128)(2,1)S(1)}, bf16[128,512]{0,1:T(8,128)(2,1)S(1)}, u32[]{:S(2)}, u32[]{:S(2)}) collective-permute-start(bf16[128,512]{0,1:T(8,128)(2,1)S(1)} %copy.41), channel_id=1, source_target_pairs={{0,7},{1,0},{2,1},{3,2},{4,3},{5,4},{6,5},{7,6},{8,15},{9,8},{10,9... | collective-permute-start | bytes 393224 | tf_op jit(solution)/shard_map/ppermute | solution.py:23
  13.0 267.4 %reduce-scatter.12.cloned.1.call-start = ((), (), s32[]{:S(2)}) async-start(), calls=%async_computation.9 | async-start | bytes 1081344 | tf_op jit(solution)/shard_map/reduce_scatter | solution.py:117
  16.8 5.6 collective-permute-start.2
  16.8 5.6 collective-permute-start.3
  22.4 5.6 collective-permute-start.4
  22.4 6.0 collective-permute-start.5
  28.0 6.5 collective-permute-start.6
  35.2 3.3 copy-start.1
  40.2 3.2 copy-start.7
  47.2 5.2 copy-start.2
  54.6 2.3 copy-start.8
  54.6 2.3 copy-start.9
  62.8 437.0 %reduce-scatter.10.cloned.1.call-start = ((), (), s32[]{:S(2)}) async-start(), calls=%async_computation.8 | async-start | bytes 1081344 | tf_op jit(solution)/shard_map/reduce_scatter | solution.py:117
  67.9 651.1 %reduce-scatter.14.cloned.1.call-start = ((), (), s32[]{:S(2)}) async-start(), calls=%async_computation.10 | async-start | bytes 1081344 | tf_op jit(solution)/shard_map/reduce_scatter | solution.py:117
  69.6 3.4 copy-start.4
  72.9 682.9 %reduce-scatter.8.cloned.1.call-start = ((), (), s32[]{:S(2)}) async-start(), calls=%async_computation.7 | async-start | bytes 1179648 | tf_op jit(solution)/shard_map/reduce_scatter | solution.py:122
  73.0 1.2 copy-start.6
  81.3 1.8 copy-start.3
  81.3 1.9 copy-start.5
  82.8 709.7 %reduce-scatter.6.cloned.1.call-start = ((), (), s32[]{:S(2)}) async-start(), calls=%async_computation.5 | async-start | bytes 1179648 | tf_op jit(solution)/shard_map/reduce_scatter | solution.py:93
Sparse Core Ops, SparseCore 0:
  13.1 27.4 all-gather.1
  62.9 217.4 reduce-scatter.11
  284.3 215.4 reduce-scatter.9
  503.5 215.4 reduce-scatter.13
  721.9 33.8 reduce-scatter.7
  758.8 33.5 reduce-scatter.5
